TPU v7x, 256 devices: a whole 4x4x8 slice. The times are simulated.
256 devices in a mesh: seg: 8 (over y, core), sec: 32 (over x, z).
Axes of the slice: x: 4, y: 4, z: 8, core: 2. Of those that a mesh axis runs over, the one named last changes fastest.
Arguments:
- psi_init: float32 [8, 32, 256, 256], P('seg', 'sec'), may hold values from -6 to 6
- boundary_env: float32 [32, 18, 256, 256], P('sec')
- right_env: float32 [8, 32, 18, 256, 256], P('seg', 'sec')
- transfer_blocks: float32 [8, 32, 256, 256], P('seg', 'sec')
- transfer_mix: float32 [8, 18, 18], P('seg')
- hop_left: float32 [8, 32, 256, 256], P('seg', 'sec'), may hold values from -0.75 to 0.75
- hop_right: float32 [8, 32, 256, 256], P('seg', 'sec'), may hold values from -0.75 to 0.75
- block_sizes: int32 [8, 2, 32], P('seg'), may hold values from 64 to 256, as said below
- sources: int32 [8, 32], P('seg'), may hold values from 0 to 31, each once within a row
Outputs:
- state: float32 [8, 32, 256, 256], P('seg', 'sec')
Inputs may be any that keep to these rules, and one draw needn't show every extreme that they name: `sources`: each block number appears once in a segment's list. `block_sizes`: each segment has a block with 256 live rows and one with 256 live columns.
All inputs are finite; a program needn't handle non-finite values.
Results may differ from a plain program's by a relative error of at most 0.0003.
Values sent between devices are 32-bit elements; how exact they have to be, the bound alone decides.
No kernel may reach another device: no remote copies, remote signals or barrier semaphores. Data moves between devices by JAX's collectives and lax.ppermute only.
A program may use at most 128 MiB of HBM per device.

v0:
```python
import jax
import jax.numpy as jnp
from jax import lax
from jax.sharding import PartitionSpec as P

DAV = 2
HIGH = lax.Precision.HIGHEST
EPSILON = 1e-06


def passed_along(value, axis, steps):
    count = lax.axis_size(axis)
    initial, last = (max(0, -steps), min(count, count - steps))
    return lax.ppermute(value, axis, [(source, source + steps) for source in range(initial, last)])


def product(left, right):
    return jnp.matmul(left, right, precision=HIGH)


def combine(earlier, later):
    return (product(earlier[0], later[0]), product(earlier[1], later[1]))


def norm_total(vector):
    return lax.psum(jnp.sum(vector * vector), "sec")


def per_device(
    psi_init,
    boundary_env,
    right_env,
    transfer_blocks,
    transfer_mix,
    hop_left,
    hop_right,
    block_sizes,
    sources,
):
    initial = psi_init[0]
    right_side = right_env[0]
    own_blocks = transfer_blocks[0]
    own_mix = transfer_mix[0]
    left_hop = hop_left[0]
    right_hop = hop_right[0]
    all_sizes = block_sizes[0]
    all_sources = sources[0]
    local_blocks = initial.shape[0]
    block_width = initial.shape[1]
    channels = own_mix.shape[0]
    sector_count = lax.axis_size("sec")
    first_block = lax.axis_index("sec") * local_blocks
    eye_mix = jnp.eye(channels, dtype=jnp.float32)
    eye_blocks = jnp.broadcast_to(jnp.eye(block_width, dtype=jnp.float32), own_blocks.shape)
    prefix_mix, prefix_blocks = (eye_mix, eye_blocks)
    leading = lax.axis_index("seg") == 0
    for hop_index in range(lax.axis_size("seg") - 1):
        carry_mix, carry_blocks = combine((prefix_mix, prefix_blocks), (own_mix, own_blocks))
        got_mix, got_blocks = passed_along((carry_mix, carry_blocks), "seg", 1)
        prefix_mix = jnp.where(leading, eye_mix, got_mix)
        prefix_blocks = jnp.where(leading, eye_blocks, got_blocks)
    turned = product(
        product(jnp.swapaxes(prefix_blocks, 1, 2)[:, None], boundary_env), prefix_blocks[:, None]
    )
    left_env = jnp.einsum("vw,bvij->bwij", prefix_mix, turned, precision=HIGH)
    live_sizes = lax.dynamic_slice_in_dim(all_sizes, first_block, local_blocks, 1)
    wanted = lax.dynamic_slice_in_dim(all_sources, first_block, local_blocks, 0)
    places = lax.broadcasted_iota(jnp.int32, (1, block_width), 1)
    row_live = (places < live_sizes[0][:, None]).astype(jnp.float32)
    col_live = (places < live_sizes[1][:, None]).astype(jnp.float32)
    masking = row_live[:, :, None] * col_live[:, None, :]
    diagonal = jnp.einsum(
        "bwi,bwj->bij",
        jnp.diagonal(left_env, axis1=2, axis2=3),
        jnp.diagonal(right_side, axis1=2, axis2=3),
        precision=HIGH,
    )
    vector = masking * initial
    vector = vector / jnp.sqrt(norm_total(vector) + EPSILON)
    for turn_index in range(DAV):
        local_part = jnp.sum(product(product(left_env, vector[:, None]), right_side), axis=1)
        moving = product(vector, right_hop)
        shard_piece = lax.all_gather(moving, "sec", axis=0, tiled=True)
        global_ids = lax.broadcasted_iota(jnp.int32, (1, shard_piece.shape[0]), 1)
        chooser = (wanted[:, None] == global_ids).astype(jnp.float32)
        regrouped = jnp.zeros_like(moving) + jnp.einsum(
            "ji,ipc->jpc", chooser, shard_piece, precision=HIGH
        )
        image_vec = masking * (local_part + product(left_hop, regrouped))
        rayleigh = lax.psum(jnp.sum(vector * image_vec), "sec")
        residue = image_vec - rayleigh * vector
        shifted = diagonal - rayleigh
        update = vector - residue * shifted / (shifted * shifted + 1.0)
        vector = update / jnp.sqrt(norm_total(update) + EPSILON)
    cells = float(local_blocks * sector_count * block_width * block_width)
    return (vector * jnp.sqrt(jnp.float32(cells)))[None]


def solution(mesh):
    return jax.shard_map(
        per_device,
        mesh=mesh,
        in_specs=(
            P("seg", "sec", None, None),
            P("sec", None, None, None),
            P("seg", "sec", None, None, None),
            P("seg", "sec", None, None),
            P("seg", None, None),
            P("seg", "sec", None, None),
            P("seg", "sec", None, None),
            P("seg", None, None),
            P("seg", None),
        ),
        out_specs=P("seg", "sec", None, None),
        check_vma=False,
    )
```

profile of v0, /device:TPU:8, one launch (start us, length us, event | category | flops | bytes accessed | tf_op | source)
XLA Modules:
  0.0 646.8 jit_solution(14586238692061087781)
XLA Ops:
  6.6 0.8 constant_dynamic-slice_fusion.1
  7.3 0.5 fusion.114
  7.9 1.2 compare_convert_fusion
  9.1 1.7 fusion.65
  10.8 78.3 %psum.35 = f32[]{:T(128)} all-reduce(f32[]{:T(128)} %fusion.65), channel_id=1, replica_groups=mesh['seg'=8,'sec'=32] {'sec'}, use_global_device_ids=true, to_apply=%region_1.2 | all-reduce | flops 1 | bytes 8 | tf_op jit(solution)/shard_map/psum | solution.py:26
  89.8 2.2 fusion.53
  92.0 0.3 convolution_bitcast_fusion.8
  92.3 1.9 collective-permute-start
  94.2 5.8 collective-permute-done
  100.0 0.4 convolution_bitcast_fusion.7
  100.4 1.9 collective-permute-start.1
  102.3 5.8 collective-permute-done.1
  108.1 0.4 convolution_bitcast_fusion.6
  108.5 1.9 collective-permute-start.2
  110.4 5.8 collective-permute-done.2
  116.2 0.4 convolution_bitcast_fusion.5
  116.6 1.9 collective-permute-start.3
  118.5 0.8 fusion.90
  119.3 3.6 collective-permute-start.7
  122.9 1.5 collective-permute-done.7
  124.4 0.8 fusion.76
  125.2 1.9 collective-permute-start.8
  127.2 0.4 convolution_bitcast_fusion.4
  127.6 3.6 collective-permute-start.4
  131.2 0.1 fusion.77
  131.3 1.9 collective-permute-start.9
  133.3 3.1 collective-permute-done.9
  136.3 0.1 fusion.78
  136.5 1.9 collective-permute-start.10
  138.4 0.4 convolution_bitcast_fusion.3
  138.8 3.3 collective-permute-start.5
  142.1 0.1 fusion.79
  142.3 1.9 collective-permute-start.11
  144.2 3.1 collective-permute-done.11
  147.5 1.9 collective-permute-start.12
  149.4 0.4 convolution_bitcast_fusion.2
  149.8 2.7 collective-permute-start.6
  152.5 0.6 constant_dynamic-slice_fusion
  153.0 18.1 %copy.26 = f32[1,1,18,256,256]{2,4,3,1,0:T(8,128)} copy(f32[1,1,18,256,256]{4,3,2,1,0:T(8,128)} %param.11) | data formatting | bytes 9437184 | tf_op args[2]
  171.1 2.4 gather_fusion.1
  173.5 0.1 fusion.81
  173.7 2.1 collective-permute-start.13
  175.8 6.1 fusion.12
  181.9 4.0 fusion.10
  186.0 10.1 %fusion.18 = f32[18,256,256]{2,0,1:T(8,128)} fusion(f32[18,256,256]{2,1,0:T(8,128)S(1)} %fusion.10, f32[18,18]{1,0:T(8,128)S(1)} %collective-permute-done.13, pred[]{:T(512)S(6)} %eq.62), kind=kOutput, calls=%fused_computation.20 | convolution fusion | flops 254804944 | bytes 9438481 | tf_op jit(solution)/shard_map/vw,bvij->bwij/dot_general | solution.py:65
  196.1 17.6 %copy.29 = f32[18,256,256]{0,2,1:T(8,128)} copy(f32[18,256,256]{2,0,1:T(8,128)} %fusion.18) | data formatting | bytes 9437184 | tf_op jit(solution)/shard_map/squeeze | solution.py:18
  213.7 2.3 gather_fusion
  216.0 7.9 %fusion.16 = f32[18,256,256]{2,1,0:T(8,128)S(1)} fusion(f32[18,256,256]{2,0,1:T(8,128)} %fusion.18, f32[1,1,256,256]{3,2,1,0:T(8,128)S(1)} %copy-done.2, f32[]{:T(128)S(6)} %sqrt.9, f32[256]{0:T(256)S(1)} %get-tuple-element.16, f32[256]{0:T(256)S(1)} %get-tuple-element.17), kind=kOutput, calls=%fused_computation.18 | convolution fusion | flops 3624075264 | bytes 9701380 | tf_op jit(solution)/shard_map/dot_general | solution.py:18
  223.9 9.9 %fusion.28 = f32[256,256]{1,0:T(8,128)S(1)} fusion(f32[18,256,256]{2,1,0:T(8,128)S(1)} %fusion.16, f32[1,1,18,256,256]{4,3,2,1,0:T(8,128)} %param.11), kind=kOutput, calls=%fused_computation.35 | convolution fusion | flops 3623878656 | bytes 9699328 | tf_op jit(solution)/shard_map/dot_general | solution.py:18
  233.9 11.0 %fusion.2 = f32[1,256,256]{2,0,1:T(1,128)S(1)} fusion(f32[32,256,256]{2,1,0:T(8,128)} %bitcast.185, s32[]{:T(128)} %bitcast.34), kind=kOutput, calls=%fused_computation.4 | convolution fusion | flops 25165856 | bytes 8650756 | tf_op jit(solution)/shard_map/ji,ipc->jpc/dot_general | solution.py:86
  244.9 1.0 multiply_reduce_fusion.3
  245.9 70.3 %psum.36 = f32[]{:T(128)} all-reduce(f32[]{:T(128)} %get-tuple-element.11), channel_id=1, replica_groups=mesh['seg'=8,'sec'=32] {'sec'}, use_global_device_ids=true, to_apply=%region_3.4 | all-reduce | flops 1 | bytes 8 | tf_op jit(solution)/shard_map/psum | solution.py:90
  316.2 1.7 multiply_reduce_fusion.2
  317.9 72.1 %psum.37 = f32[]{:T(128)} all-reduce(f32[]{:T(128)} %get-tuple-element.7), channel_id=1, replica_groups=mesh['seg'=8,'sec'=32] {'sec'}, use_global_device_ids=true, to_apply=%region_5.6 | all-reduce | flops 1 | bytes 8 | tf_op jit(solution)/shard_map/psum | solution.py:26
  390.8 1.1 fusion.51
  391.9 7.8 %fusion.14 = f32[18,256,256]{2,1,0:T(8,128)S(1)} fusion(f32[18,256,256]{2,0,1:T(8,128)} %fusion.18, f32[256,256]{1,0:T(8,128)S(1)} %get-tuple-element.8, f32[]{:T(128)S(6)} %sqrt.10), kind=kOutput, calls=%fused_computation.16 | convolution fusion | flops 3623944192 | bytes 9699332 | tf_op jit(solution)/shard_map/dot_general | solution.py:18
  399.7 4.1 fusion.25
  403.8 78.8 %all-gather.7.cloned.1.call-done = f32[8192,256]{1,0:T(8,128)} async-done(((f32[256,256]{1,0:T(8,128)}), f32[8192,256]{1,0:T(8,128)}) %all-gather.7.cloned.1.call-update) | async-done | bytes 8388624 | tf_op jit(solution)/shard_map/all_gather | solution.py:83
  482.6 11.0 %fusion = f32[1,256,256]{2,0,1:T(1,128)S(1)} fusion(f32[32,256,256]{2,1,0:T(8,128)} %bitcast.186, s32[]{:T(128)} %bitcast.34), kind=kOutput, calls=%fused_computation.2 | convolution fusion | flops 25165856 | bytes 8650756 | tf_op jit(solution)/shard_map/ji,ipc->jpc/dot_general | solution.py:86
  493.7 1.0 multiply_reduce_fusion.1
  494.7 71.9 %psum.38 = f32[]{:T(128)} all-reduce(f32[]{:T(128)} %get-tuple-element.14), channel_id=1, replica_groups=mesh['seg'=8,'sec'=32] {'sec'}, use_global_device_ids=true, to_apply=%region_7.8 | all-reduce | flops 1 | bytes 8 | tf_op jit(solution)/shard_map/psum | solution.py:90
  566.6 1.3 multiply_reduce_fusion
  567.9 70.5 %psum.39 = f32[]{:T(128)} all-reduce(f32[]{:T(128)} %get-tuple-element.5), channel_id=1, replica_groups=mesh['seg'=8,'sec'=32] {'sec'}, use_global_device_ids=true, to_apply=%region_9.10 | all-reduce | flops 1 | bytes 8 | tf_op jit(solution)/shard_map/psum | solution.py:26
  639.1 0.7 multiply_bitcast_fusion
  (34 shorter events, 0.3 us)
Async XLA Ops:
  6.5 85.4 %copy-start = (f32[1,1,256,256]{3,2,1,0:T(8,128)S(1)}, f32[1,1,256,256]{3,2,1,0:T(8,128)}, u32[]{:S(2)}) copy-start(f32[1,1,256,256]{3,2,1,0:T(8,128)} %param.12) | copy-start | bytes 786436
  6.5 124.6 %copy-start.3 = (f32[1,18,18]{2,0,1:T(1,128)S(1)}, f32[1,18,18]{2,0,1:T(1,128)}, u32[]{:S(2)}) copy-start(f32[1,18,18]{2,0,1:T(1,128)} %param.13) | copy-start | bytes 3892
  6.5 145.9 %copy-start.6 = (s32[1,32]{1,0:T(1,128)S(1)}, s32[1,32]{1,0:T(1,128)}, u32[]{:S(2)}) copy-start(s32[1,32]{1,0:T(1,128)} %param.17) | copy-start | bytes 388
  6.5 227.3 %all-gather.5.cloned.1.call-start = ((), (), s32[]{:S(2)}) async-start(), calls=%async_computation | async-start | bytes 8650752 | tf_op jit(solution)/shard_map/all_gather | solution.py:83
  91.9 390.7 %all-gather.7.cloned.1.call-start = ((), (), s32[]{:S(2)}) async-start(), calls=%async_computation.1 | async-start | bytes 8650752 | tf_op jit(solution)/shard_map/all_gather | solution.py:83
  92.3 7.7 %collective-permute-start = (f32[1,256,256]{2,1,0:T(8,128)S(1)}, f32[1,256,256]{2,1,0:T(8,128)S(1)}, u32[]{:S(2)}, u32[]{:S(2)}) collective-permute-start(f32[1,256,256]{2,1,0:T(8,128)S(1)} %convolution_bitcast_fusion.8), channel_id=1, source_target_pairs={{0,32},{32,64},{64,96},{96,128},{128,160},{160,192},{192,224},{1,3... | collective-permute-start | bytes 786440 | tf_op jit(solution)/shard_map/ppermute | solution.py:14
  100.4 7.7 %collective-permute-start.1 = (f32[1,256,256]{2,1,0:T(8,128)S(1)}, f32[1,256,256]{2,1,0:T(8,128)S(1)}, u32[]{:S(2)}, u32[]{:S(2)}) collective-permute-start(f32[1,256,256]{2,1,0:T(8,128)S(1)} %convolution_bitcast_fusion.7), channel_id=1, source_target_pairs={{0,32},{32,64},{64,96},{96,128},{128,160},{160,192},{192,224},{1,3... | collective-permute-start | bytes 786440 | tf_op jit(solution)/shard_map/ppermute | solution.py:14
  108.5 7.7 %collective-permute-start.2 = (f32[1,256,256]{2,1,0:T(8,128)S(1)}, f32[1,256,256]{2,1,0:T(8,128)S(1)}, u32[]{:S(2)}, u32[]{:S(2)}) collective-permute-start(f32[1,256,256]{2,1,0:T(8,128)S(1)} %convolution_bitcast_fusion.6), channel_id=1, source_target_pairs={{0,32},{32,64},{64,96},{96,128},{128,160},{160,192},{192,224},{1,3... | collective-permute-start | bytes 786440 | tf_op jit(solution)/shard_map/ppermute | solution.py:14
  116.6 10.6 %collective-permute-start.3 = (f32[1,256,256]{2,1,0:T(8,128)S(1)}, f32[1,256,256]{2,1,0:T(8,128)S(1)}, u32[]{:S(2)}, u32[]{:S(2)}) collective-permute-start(f32[1,256,256]{2,1,0:T(8,128)S(1)} %convolution_bitcast_fusion.5), channel_id=1, source_target_pairs={{0,32},{32,64},{64,96},{96,128},{128,160},{160,192},{192,224},{1,3... | collective-permute-start | bytes 786440 | tf_op jit(solution)/shard_map/ppermute | solution.py:14
  119.3 5.1 collective-permute-start.7
  125.2 5.9 collective-permute-start.8
  127.6 10.9 %collective-permute-start.4 = (f32[1,256,256]{2,1,0:T(8,128)S(1)}, f32[1,256,256]{2,1,0:T(8,128)S(1)}, u32[]{:S(2)}, u32[]{:S(2)}) collective-permute-start(f32[1,256,256]{2,1,0:T(8,128)S(1)} %convolution_bitcast_fusion.4), channel_id=1, source_target_pairs={{0,32},{32,64},{64,96},{96,128},{128,160},{160,192},{192,224},{1,3... | collective-permute-start | bytes 786440 | tf_op jit(solution)/shard_map/ppermute | solution.py:14
  131.3 5.0 collective-permute-start.9
  136.5 5.6 collective-permute-start.10
  138.8 10.6 %collective-permute-start.5 = (f32[1,256,256]{2,1,0:T(8,128)S(1)}, f32[1,256,256]{2,1,0:T(8,128)S(1)}, u32[]{:S(2)}, u32[]{:S(2)}) collective-permute-start(f32[1,256,256]{2,1,0:T(8,128)S(1)} %convolution_bitcast_fusion.3), channel_id=1, source_target_pairs={{0,32},{32,64},{64,96},{96,128},{128,160},{160,192},{192,224},{1,3... | collective-permute-start | bytes 786440 | tf_op jit(solution)/shard_map/ppermute | solution.py:14
  142.3 5.0 collective-permute-start.11
  147.5 26.1 %collective-permute-start.12 = (f32[18,18]{1,0:T(8,128)S(1)}, f32[18,18]{1,0:T(8,128)S(1)}, u32[]{:S(2)}, u32[]{:S(2)}) collective-permute-start(f32[18,18]{1,0:T(8,128)S(1)} %fusion.80), channel_id=1, source_target_pairs={{0,32},{32,64},{64,96},{96,128},{128,160},{160,192},{192,224},{1,3... | collective-permute-start | bytes 3896 | tf_op jit(solution)/shard_map/ppermute | solution.py:14
  149.8 26.0 %collective-permute-start.6 = (f32[1,256,256]{2,1,0:T(8,128)S(1)}, f32[1,256,256]{2,1,0:T(8,128)S(1)}, u32[]{:S(2)}, u32[]{:S(2)}) collective-permute-start(f32[1,256,256]{2,1,0:T(8,128)S(1)} %convolution_bitcast_fusion.2), channel_id=1, source_target_pairs={{0,32},{32,64},{64,96},{96,128},{128,160},{160,192},{192,224},{1,3... | collective-permute-start | bytes 786440 | tf_op jit(solution)/shard_map/ppermute | solution.py:14
  173.7 12.3 %collective-permute-start.13 = (f32[18,18]{1,0:T(8,128)S(1)}, f32[18,18]{1,0:T(8,128)S(1)}, u32[]{:S(2)}, u32[]{:S(2)}) collective-permute-start(f32[18,18]{1,0:T(8,128)S(1)} %fusion.81), channel_id=1, source_target_pairs={{0,32},{32,64},{64,96},{96,128},{128,160},{160,192},{192,224},{1,3... | collective-permute-start | bytes 3896 | tf_op jit(solution)/shard_map/ppermute | solution.py:14
  196.1 20.0 %copy-start.2 = (f32[1,1,256,256]{3,2,1,0:T(8,128)S(1)}, f32[1,1,256,256]{3,2,1,0:T(8,128)}, u32[]{:S(2)}) copy-start(f32[1,1,256,256]{3,2,1,0:T(8,128)} %param.9) | copy-start | bytes 786436
  233.8 11.1 %copy-start.5 = (f32[1,1,256,256]{3,2,1,0:T(8,128)S(1)}, f32[1,1,256,256]{3,2,1,0:T(8,128)}, u32[]{:S(2)}) copy-start(f32[1,1,256,256]{3,2,1,0:T(8,128)} %param.14) | copy-start | bytes 786436
  233.9 156.9 %copy-start.4 = (f32[1,1,256,256]{3,2,1,0:T(8,128)S(1)}, f32[1,1,256,256]{3,2,1,0:T(8,128)}, u32[]{:S(2)}) copy-start(f32[1,1,256,256]{3,2,1,0:T(8,128)} %param.15) | copy-start | bytes 786436
  316.2 83.5 %slice-start = ((s8[4718592]{0:T(1024)(128)(4,1)}), s8[524288]{0:T(1024)(128)(4,1)S(1)}, s32[]{:S(2)}) async-start(s8[4718592]{0:T(1024)(128)(4,1)} %bitcast.182), calls=%async_computation.2 | async-start | bytes 1048576
  391.9 7.8 %slice-start.1 = ((s8[4718592]{0:T(1024)(128)(4,1)}), s8[4194304]{0:T(1024)(128)(4,1)S(1)}, s32[]{:S(2)}) async-start(s8[4718592]{0:T(1024)(128)(4,1)} %bitcast.182), calls=%async_computation.3 | async-start | bytes 8388608
  482.6 157.2 %copy-start.1 = (f32[1,1,256,256]{3,2,1,0:T(8,128)S(1)}, f32[1,1,256,256]{3,2,1,0:T(8,128)}, u32[]{:S(2)}) copy-start(f32[1,1,256,256]{3,2,1,0:T(8,128)} %param.12) | copy-start | bytes 786436
Sparse Core Ops, SparseCore 0:
  92.1 91.5 all-gather.4
  392.0 90.6 all-gather.6
where the time goes:
time: 653 us; the launch traced here: 647 us
  blocking collectives  363 us (56%)
  waiting for transfers between devices  104 us (16%)
  matrix products  84 us (13%)
  local copies, waits for them, and re-layouts  42.3 us (6%)
  starting transfers between devices  32.6 us (5%)
  between operations  16.1 us (2%)
    psum x3, blocking collectives, norm_total(): return lax.psum(jnp.sum(vector * vector), 'sec')  221 us
    psum x2, blocking collectives, per_device(): rayleigh = lax.psum(jnp.sum(vector * image_vec), 'sec')  142 us
    all_gather x2, waiting for transfers between devices, per_device(): shard_piece = lax.all_gather(moving, 'sec', axis=0, tiled=True)  78.9 us
    dot_general x24, matrix products, product(): return jnp.matmul(left, right, precision=HIGH)  50 us
    ppermute x14, starting transfers between devices, passed_along(): lax.ppermute(value, axis, [(source, source + steps) for source in range(i...  32.5 us
    ppermute x14, waiting for transfers between devices, passed_along(): lax.ppermute(value, axis, [(source, source + steps) for source in range(i...  24.9 us
    dot_general x2, matrix products, per_device(): jnp.einsum('ji,ipc->jpc', chooser, shard_piece, precision=HIGH)  22 us
    unnamed x19, local copies, waits for them, and re-layouts  18.1 us
  transfers between devices with their start and end apart: 16, of which 7 were waited for; matrix products, arithmetic and copies ran while one was open for 15% of the time, Pallas kernels for 0%

commit v1 on v0

--- a/solution.py
+++ b/solution.py
@@ -1,3 +1,4 @@
+import functools
 import jax
 import jax.numpy as jnp
 from jax import lax
@@ -6,6 +7,17 @@
 DAV = 2
 HIGH = lax.Precision.HIGHEST
 EPSILON = 1e-06
+
+
+def assign_grid(inputs, axis_k):
+    ledger = []
+    for _ in range(lax.axis_size("sec")):
+        ledger.append(inputs)
+    built = lax.all_to_all(jnp.stack(ledger), "sec", 0, 0)
+    return jnp.concatenate(built, axis=axis_k)
+
+
+recover_ladders = functools.partial(assign_grid, axis_k=0)
 
 
 def passed_along(value, axis, steps):
@@ -80,7 +92,7 @@
     for turn_index in range(DAV):
         local_part = jnp.sum(product(product(left_env, vector[:, None]), right_side), axis=1)
         moving = product(vector, right_hop)
-        shard_piece = lax.all_gather(moving, "sec", axis=0, tiled=True)
+        shard_piece = recover_ladders(moving)
         global_ids = lax.broadcasted_iota(jnp.int32, (1, shard_piece.shape[0]), 1)
         chooser = (wanted[:, None] == global_ids).astype(jnp.float32)
         regrouped = jnp.zeros_like(moving) + jnp.einsum(

time: 653 us -> 747 us (1.14)
  waiting for transfers between devices: 104 us -> 184 us
  between operations: 16.1 us -> 3.03 us
  starting transfers between devices: 32.6 us -> 44.3 us
  local copies, waits for them, and re-layouts: 42.3 us -> 50.6 us
    all_to_all x0 -> x2, waiting for transfers between devices: none -> 158 us  [assign_grid(): built = lax.all_to_all(jnp.stack(ledger), 'sec', 0, 0)]
    all_gather x2 -> x0, waiting for transfers between devices: 78.9 us -> none  [per_device(): shard_piece = lax.all_gather(moving, 'sec', axis=0, tiled=True)]
    all_to_all x0 -> x2, starting transfers between devices: none -> 11.5 us  [assign_grid(): built = lax.all_to_all(jnp.stack(ledger), 'sec', 0, 0)]
    another operation x0 -> x2, local copies, waits for them, and re-layouts: none -> 8.31 us  [assign_grid(): built = lax.all_to_all(jnp.stack(ledger), 'sec', 0, 0)]
    unnamed x19 -> x15, local copies, waits for them, and re-layouts: 18.1 us -> 18.1 us
  transfers between devices with their start and end apart: 16 -> 16, of which waited for: 7 -> 8; matrix products, arithmetic and copies ran while one was open for 15% -> 13% of each run, Pallas kernels for 0% -> 0%
where the time goes in v1:
time: 747 us; the launch traced here: 740 us
  blocking collectives  366 us (49%)
  waiting for transfers between devices  184 us (25%)
  matrix products  86.6 us (12%)
  local copies, waits for them, and re-layouts  50.6 us (7%)
  starting transfers between devices  44.3 us (6%)
    psum x3, blocking collectives, norm_total(): return lax.psum(jnp.sum(vector * vector), 'sec')  224 us
    all_to_all x2, waiting for transfers between devices, assign_grid(): built = lax.all_to_all(jnp.stack(ledger), 'sec', 0, 0)  158 us
    psum x2, blocking collectives, per_device(): rayleigh = lax.psum(jnp.sum(vector * image_vec), 'sec')  142 us
    dot_general x24, matrix products, product(): return jnp.matmul(left, right, precision=HIGH)  52.4 us
    ppermute x14, starting transfers between devices, passed_along(): lax.ppermute(value, axis, [(source, source + steps) for source in range(i...  32.9 us
    ppermute x14, waiting for transfers between devices, passed_along(): lax.ppermute(value, axis, [(source, source + steps) for source in range(i...  25.6 us
    dot_general x2, matrix products, per_device(): jnp.einsum('ji,ipc->jpc', chooser, shard_piece, precision=HIGH)  22.2 us
    unnamed x15, local copies, waits for them, and re-layouts  18.1 us
  transfers between devices with their start and end apart: 16, of which 8 were waited for; matrix products, arithmetic and copies ran while one was open for 13% of the time, Pallas kernels for 0%

profile of v1, /device:TPU:8, one launch (start us, length us, event | category | flops | bytes accessed | tf_op | source)
XLA Modules:
  0.0 739.9 jit_solution(1678159028273070738)
XLA Ops:
  0.0 0.8 constant_dynamic-slice_fusion.1
  0.8 0.5 fusion.114
  1.3 1.3 compare_convert_fusion
  2.6 1.7 fusion.65
  4.3 78.3 %psum.35 = f32[]{:T(128)} all-reduce(f32[]{:T(128)} %fusion.65), channel_id=1, replica_groups=mesh['seg'=8,'sec'=32] {'sec'}, use_global_device_ids=true, to_apply=%region_1.2 | all-reduce | flops 1 | bytes 8 | tf_op jit(solution)/shard_map/psum | solution.py:38
  83.3 1.4 fusion.53
  84.8 4.1 stack.6
  88.9 5.1 all-to-all-start
  94.0 0.3 convolution_bitcast_fusion.8
  94.3 1.9 collective-permute-start
  96.3 5.8 collective-permute-done
  102.0 0.4 convolution_bitcast_fusion.7
  102.4 1.9 collective-permute-start.1
  104.4 5.8 collective-permute-done.1
  110.1 0.4 convolution_bitcast_fusion.6
  110.5 1.9 collective-permute-start.2
  112.5 5.8 collective-permute-done.2
  118.2 0.4 convolution_bitcast_fusion.5
  118.6 1.9 collective-permute-start.3
  120.7 3.6 collective-permute-start.7
  124.3 2.2 collective-permute-done.7
  126.6 1.9 collective-permute-start.8
  128.5 0.4 convolution_bitcast_fusion.4
  128.9 3.6 collective-permute-start.4
  132.7 1.9 collective-permute-start.9
  134.6 3.1 collective-permute-done.9
  137.8 1.9 collective-permute-start.10
  139.8 0.4 convolution_bitcast_fusion.3
  140.2 3.3 collective-permute-start.5
  143.5 0.1 fusion.79
  143.6 1.9 collective-permute-start.11
  145.6 3.1 collective-permute-done.11
  148.8 1.9 collective-permute-start.12
  150.7 0.4 convolution_bitcast_fusion.2
  151.1 2.7 collective-permute-start.6
  153.8 0.6 constant_dynamic-slice_fusion
  154.4 18.1 %copy.26 = f32[1,1,18,256,256]{2,4,3,1,0:T(8,128)} copy(f32[1,1,18,256,256]{4,3,2,1,0:T(8,128)} %param.11) | data formatting | bytes 9437184 | tf_op args[2]
  172.5 2.3 gather_fusion.1
  175.0 2.4 collective-permute-start.13
  177.5 6.1 fusion.12
  183.6 4.0 fusion.10
  187.6 10.2 %fusion.18 = f32[18,256,256]{2,0,1:T(8,128)} fusion(f32[18,256,256]{2,1,0:T(8,128)S(1)} %fusion.10, f32[18,18]{1,0:T(8,128)S(1)} %collective-permute-done.13, pred[]{:T(512)S(6)} %eq.81), kind=kOutput, calls=%fused_computation.20 | convolution fusion | flops 254804944 | bytes 9438481 | tf_op jit(solution)/shard_map/vw,bvij->bwij/dot_general | solution.py:77
  197.8 17.6 %copy.29 = f32[18,256,256]{0,2,1:T(8,128)} copy(f32[18,256,256]{2,0,1:T(8,128)} %fusion.18) | data formatting | bytes 9437184 | tf_op jit(solution)/shard_map/squeeze | solution.py:30
  215.4 2.3 gather_fusion
  217.8 7.8 %fusion.16 = f32[18,256,256]{2,1,0:T(8,128)S(1)} fusion(f32[18,256,256]{2,0,1:T(8,128)} %fusion.18, f32[1,1,256,256]{3,2,1,0:T(8,128)S(1)} %copy-done.2, f32[]{:T(128)S(6)} %sqrt.9, f32[256]{0:T(256)S(1)} %get-tuple-element.16, f32[256]{0:T(256)S(1)} %get-tuple-element.17), kind=kOutput, calls=%fused_computation.18 | convolution fusion | flops 3624075264 | bytes 9701380 | tf_op jit(solution)/shard_map/dot_general | solution.py:30
  225.6 9.7 %fusion.28 = f32[256,256]{1,0:T(8,128)S(1)} fusion(f32[18,256,256]{2,1,0:T(8,128)S(1)} %fusion.16, f32[1,1,18,256,256]{4,3,2,1,0:T(8,128)} %param.11), kind=kOutput, calls=%fused_computation.35 | convolution fusion | flops 3623878656 | bytes 9699328 | tf_op jit(solution)/shard_map/dot_general | solution.py:30
  235.3 32.0 %all-to-all-done = f32[32,1,256,256]{3,2,1,0:T(8,128)} async-done(((f32[32,1,256,256]{3,2,1,0:T(8,128)}), f32[32,1,256,256]{3,2,1,0:T(8,128)}, u32[]{:S(2)}, u32[]{:S(2)}) %all-to-all-start) | async-done | bytes 8388640 | tf_op jit(solution)/shard_map/all_to_all | solution.py:16
  267.3 11.1 %fusion.2 = f32[1,256,256]{2,0,1:T(1,128)S(1)} fusion(f32[32,256,256]{2,1,0:T(8,128)} %bitcast.38, s32[]{:T(128)} %bitcast.34), kind=kOutput, calls=%fused_computation.4 | convolution fusion | flops 25165856 | bytes 8650756 | tf_op jit(solution)/shard_map/ji,ipc->jpc/dot_general | solution.py:98
  278.4 1.1 multiply_reduce_fusion.3
  279.5 70.7 %psum.36 = f32[]{:T(128)} all-reduce(f32[]{:T(128)} %get-tuple-element.11), channel_id=1, replica_groups=mesh['seg'=8,'sec'=32] {'sec'}, use_global_device_ids=true, to_apply=%region_3.4 | all-reduce | flops 1 | bytes 8 | tf_op jit(solution)/shard_map/psum | solution.py:102
  350.2 1.7 multiply_reduce_fusion.2
  352.0 74.7 %psum.37 = f32[]{:T(128)} all-reduce(f32[]{:T(128)} %get-tuple-element.7), channel_id=1, replica_groups=mesh['seg'=8,'sec'=32] {'sec'}, use_global_device_ids=true, to_apply=%region_5.6 | all-reduce | flops 1 | bytes 8 | tf_op jit(solution)/shard_map/psum | solution.py:38
  427.4 0.4 fusion.51
  427.8 4.2 stack.7
  431.9 6.4 all-to-all-start.1
  438.3 7.5 %fusion.14 = f32[18,256,256]{2,1,0:T(8,128)S(1)} fusion(f32[18,256,256]{2,0,1:T(8,128)} %fusion.18, f32[256,256]{1,0:T(8,128)S(1)} %get-tuple-element.8, f32[]{:T(128)S(6)} %sqrt.10), kind=kOutput, calls=%fused_computation.16 | convolution fusion | flops 3623944192 | bytes 9699332 | tf_op jit(solution)/shard_map/dot_general | solution.py:30
  445.8 9.8 %fusion.25 = f32[256,256]{1,0:T(8,128)S(1)} fusion(f32[18,256,256]{2,1,0:T(8,128)S(1)} %fusion.14, f32[1,1,18,256,256]{4,3,2,1,0:T(8,128)} %param.11), kind=kOutput, calls=%fused_computation.34 | convolution fusion | flops 3623878656 | bytes 9699328 | tf_op jit(solution)/shard_map/dot_general | solution.py:30
  455.6 126.5 %all-to-all-done.1 = f32[32,1,256,256]{3,2,1,0:T(8,128)} async-done(((f32[32,1,256,256]{3,2,1,0:T(8,128)}), f32[32,1,256,256]{3,2,1,0:T(8,128)}, u32[]{:S(2)}, u32[]{:S(2)}) %all-to-all-start.1) | async-done | bytes 8388640 | tf_op jit(solution)/shard_map/all_to_all | solution.py:16
  582.1 11.1 %fusion = f32[1,256,256]{2,0,1:T(1,128)S(1)} fusion(f32[32,256,256]{2,1,0:T(8,128)} %bitcast.49, s32[]{:T(128)} %bitcast.34), kind=kOutput, calls=%fused_computation.2 | convolution fusion | flops 25165856 | bytes 8650756 | tf_op jit(solution)/shard_map/ji,ipc->jpc/dot_general | solution.py:98
  593.2 1.0 multiply_reduce_fusion.1
  594.2 71.6 %psum.38 = f32[]{:T(128)} all-reduce(f32[]{:T(128)} %get-tuple-element.14), channel_id=1, replica_groups=mesh['seg'=8,'sec'=32] {'sec'}, use_global_device_ids=true, to_apply=%region_7.8 | all-reduce | flops 1 | bytes 8 | tf_op jit(solution)/shard_map/psum | solution.py:102
  665.7 1.4 multiply_reduce_fusion
  667.1 70.8 %psum.39 = f32[]{:T(128)} all-reduce(f32[]{:T(128)} %get-tuple-element.5), channel_id=1, replica_groups=mesh['seg'=8,'sec'=32] {'sec'}, use_global_device_ids=true, to_apply=%region_9.10 | all-reduce | flops 1 | bytes 8 | tf_op jit(solution)/shard_map/psum | solution.py:38
  738.6 0.7 multiply_bitcast_fusion
  (29 shorter events, 0.9 us)
Async XLA Ops:
  0.0 94.0 %copy-start = (f32[1,1,256,256]{3,2,1,0:T(8,128)S(1)}, f32[1,1,256,256]{3,2,1,0:T(8,128)}, u32[]{:S(2)}) copy-start(f32[1,1,256,256]{3,2,1,0:T(8,128)} %param.12) | copy-start | bytes 786436
  88.9 31.6 %copy-start.3 = (f32[1,18,18]{2,0,1:T(1,128)S(1)}, f32[1,18,18]{2,0,1:T(1,128)}, u32[]{:S(2)}) copy-start(f32[1,18,18]{2,0,1:T(1,128)} %param.13) | copy-start | bytes 3892
  88.9 178.4 %all-to-all-start = ((f32[32,1,256,256]{3,2,1,0:T(8,128)}), f32[32,1,256,256]{3,2,1,0:T(8,128)}, u32[]{:S(2)}, u32[]{:S(2)}) async-start(f32[32,1,256,256]{3,2,1,0:T(8,128)} %stack.6), calls=%async_computation | async-start | bytes 16777216 | tf_op jit(solution)/shard_map/all_to_all | solution.py:16
  94.0 59.8 %copy-start.6 = (s32[1,32]{1,0:T(1,128)S(1)}, s32[1,32]{1,0:T(1,128)}, u32[]{:S(2)}) copy-start(s32[1,32]{1,0:T(1,128)} %param.17) | copy-start | bytes 388
  94.3 7.7 %collective-permute-start = (f32[1,256,256]{2,1,0:T(8,128)S(1)}, f32[1,256,256]{2,1,0:T(8,128)S(1)}, u32[]{:S(2)}, u32[]{:S(2)}) collective-permute-start(f32[1,256,256]{2,1,0:T(8,128)S(1)} %convolution_bitcast_fusion.8), channel_id=1, source_target_pairs={{0,32},{32,64},{64,96},{96,128},{128,160},{160,192},{192,224},{1,3... | collective-permute-start | bytes 786440 | tf_op jit(solution)/shard_map/ppermute | solution.py:26
  102.4 7.7 %collective-permute-start.1 = (f32[1,256,256]{2,1,0:T(8,128)S(1)}, f32[1,256,256]{2,1,0:T(8,128)S(1)}, u32[]{:S(2)}, u32[]{:S(2)}) collective-permute-start(f32[1,256,256]{2,1,0:T(8,128)S(1)} %convolution_bitcast_fusion.7), channel_id=1, source_target_pairs={{0,32},{32,64},{64,96},{96,128},{128,160},{160,192},{192,224},{1,3... | collective-permute-start | bytes 786440 | tf_op jit(solution)/shard_map/ppermute | solution.py:26
  110.5 7.7 %collective-permute-start.2 = (f32[1,256,256]{2,1,0:T(8,128)S(1)}, f32[1,256,256]{2,1,0:T(8,128)S(1)}, u32[]{:S(2)}, u32[]{:S(2)}) collective-permute-start(f32[1,256,256]{2,1,0:T(8,128)S(1)} %convolution_bitcast_fusion.6), channel_id=1, source_target_pairs={{0,32},{32,64},{64,96},{96,128},{128,160},{160,192},{192,224},{1,3... | collective-permute-start | bytes 786440 | tf_op jit(solution)/shard_map/ppermute | solution.py:26
  118.6 9.9 %collective-permute-start.3 = (f32[1,256,256]{2,1,0:T(8,128)S(1)}, f32[1,256,256]{2,1,0:T(8,128)S(1)}, u32[]{:S(2)}, u32[]{:S(2)}) collective-permute-start(f32[1,256,256]{2,1,0:T(8,128)S(1)} %convolution_bitcast_fusion.5), channel_id=1, source_target_pairs={{0,32},{32,64},{64,96},{96,128},{128,160},{160,192},{192,224},{1,3... | collective-permute-start | bytes 786440 | tf_op jit(solution)/shard_map/ppermute | solution.py:26
  120.7 5.8 collective-permute-start.7
  126.6 5.9 collective-permute-start.8
  128.9 10.8 %collective-permute-start.4 = (f32[1,256,256]{2,1,0:T(8,128)S(1)}, f32[1,256,256]{2,1,0:T(8,128)S(1)}, u32[]{:S(2)}, u32[]{:S(2)}) collective-permute-start(f32[1,256,256]{2,1,0:T(8,128)S(1)} %convolution_bitcast_fusion.4), channel_id=1, source_target_pairs={{0,32},{32,64},{64,96},{96,128},{128,160},{160,192},{192,224},{1,3... | collective-permute-start | bytes 786440 | tf_op jit(solution)/shard_map/ppermute | solution.py:26
  132.7 5.0 collective-permute-start.9
  137.8 5.6 collective-permute-start.10
  140.2 10.6 %collective-permute-start.5 = (f32[1,256,256]{2,1,0:T(8,128)S(1)}, f32[1,256,256]{2,1,0:T(8,128)S(1)}, u32[]{:S(2)}, u32[]{:S(2)}) collective-permute-start(f32[1,256,256]{2,1,0:T(8,128)S(1)} %convolution_bitcast_fusion.3), channel_id=1, source_target_pairs={{0,32},{32,64},{64,96},{96,128},{128,160},{160,192},{192,224},{1,3... | collective-permute-start | bytes 786440 | tf_op jit(solution)/shard_map/ppermute | solution.py:26
  143.6 5.0 collective-permute-start.11
  148.8 26.0 %collective-permute-start.12 = (f32[18,18]{1,0:T(8,128)S(1)}, f32[18,18]{1,0:T(8,128)S(1)}, u32[]{:S(2)}, u32[]{:S(2)}) collective-permute-start(f32[18,18]{1,0:T(8,128)S(1)} %fusion.80), channel_id=1, source_target_pairs={{0,32},{32,64},{64,96},{96,128},{128,160},{160,192},{192,224},{1,3... | collective-permute-start | bytes 3896 | tf_op jit(solution)/shard_map/ppermute | solution.py:26
  151.1 26.3 %collective-permute-start.6 = (f32[1,256,256]{2,1,0:T(8,128)S(1)}, f32[1,256,256]{2,1,0:T(8,128)S(1)}, u32[]{:S(2)}, u32[]{:S(2)}) collective-permute-start(f32[1,256,256]{2,1,0:T(8,128)S(1)} %convolution_bitcast_fusion.2), channel_id=1, source_target_pairs={{0,32},{32,64},{64,96},{96,128},{128,160},{160,192},{192,224},{1,3... | collective-permute-start | bytes 786440 | tf_op jit(solution)/shard_map/ppermute | solution.py:26
  175.0 12.6 %collective-permute-start.13 = (f32[18,18]{1,0:T(8,128)S(1)}, f32[18,18]{1,0:T(8,128)S(1)}, u32[]{:S(2)}, u32[]{:S(2)}) collective-permute-start(f32[18,18]{1,0:T(8,128)S(1)} %fusion.81), channel_id=1, source_target_pairs={{0,32},{32,64},{64,96},{96,128},{128,160},{160,192},{192,224},{1,3... | collective-permute-start | bytes 3896 | tf_op jit(solution)/shard_map/ppermute | solution.py:26
  197.8 20.0 %copy-start.2 = (f32[1,1,256,256]{3,2,1,0:T(8,128)S(1)}, f32[1,1,256,256]{3,2,1,0:T(8,128)}, u32[]{:S(2)}) copy-start(f32[1,1,256,256]{3,2,1,0:T(8,128)} %param.9) | copy-start | bytes 786436
  235.3 43.1 %copy-start.5 = (f32[1,1,256,256]{3,2,1,0:T(8,128)S(1)}, f32[1,1,256,256]{3,2,1,0:T(8,128)}, u32[]{:S(2)}) copy-start(f32[1,1,256,256]{3,2,1,0:T(8,128)} %param.14) | copy-start | bytes 786436
  267.3 160.1 %copy-start.4 = (f32[1,1,256,256]{3,2,1,0:T(8,128)S(1)}, f32[1,1,256,256]{3,2,1,0:T(8,128)}, u32[]{:S(2)}) copy-start(f32[1,1,256,256]{3,2,1,0:T(8,128)} %param.15) | copy-start | bytes 786436
  431.9 150.1 %all-to-all-start.1 = ((f32[32,1,256,256]{3,2,1,0:T(8,128)}), f32[32,1,256,256]{3,2,1,0:T(8,128)}, u32[]{:S(2)}, u32[]{:S(2)}) async-start(f32[32,1,256,256]{3,2,1,0:T(8,128)} %stack.7), calls=%async_computation.1 | async-start | bytes 16777216 | tf_op jit(solution)/shard_map/all_to_all | solution.py:16
  582.1 157.3 %copy-start.1 = (f32[1,1,256,256]{3,2,1,0:T(8,128)S(1)}, f32[1,1,256,256]{3,2,1,0:T(8,128)}, u32[]{:S(2)}) copy-start(f32[1,1,256,256]{3,2,1,0:T(8,128)} %param.12) | copy-start | bytes 786436
